TPU v7x, 32 devices: a whole 2x2x4 slice. The times are simulated.
32 devices in a mesh: grp: 2 (over x), blk: 16 (over z, y, core).
Axes of the slice: x: 2, y: 2, z: 4, core: 2. Of those that a mesh axis runs over, the one named last changes fastest.
Arguments:
- tokens: bfloat16 [16384, 1024], P(('grp', 'blk')), parts along dimension 0, may hold values from -6 to 6
- patch_of_row: int32 [16384], P(('grp', 'blk')), parts along dimension 0, may hold values from 0 to 2047, as said below
- latents: bfloat16 [256, 1024], P('blk'), may hold values from -110 to 110
- contrast_gain: bfloat16 [4, 1024], replicated, may hold values from 0.099609375 to 1.8984375
- norm_gain: bfloat16 [1024], replicated, may hold values from 0.099609375 to 1.8984375
- w_query: bfloat16 [1024, 1024], replicated, may hold values from -0.1875 to 0.1875
- w_key: bfloat16 [1024, 1024], replicated, may hold values from -0.1875 to 0.1875
- w_value: bfloat16 [1024, 1024], replicated, may hold values from -0.1875 to 0.1875
- w_out: bfloat16 [1024, 1024], replicated, may hold values from -0.1875 to 0.1875
Outputs:
- new_latents: bfloat16 [512, 1024], P(('grp', 'blk')), parts along dimension 0
There are 2 independent parts, one for each index of `grp`. A program takes and returns all parts, laid end to end along the dimension named above; an argument that names none is the same for every part. Nothing has to cross between parts.
Inputs may be any that keep to these rules, and one draw needn't show every extreme that they name: `patch_of_row`: for each contrast c, rows c * 2048 to (c + 1) * 2048 - 1 name every patch once, and row c * 2048 + s names a patch p with p // 128 == s % 16.
All inputs are finite; a program needn't handle non-finite values.
Results may differ from a plain program's by a relative error of at most 0.0065.
Values may be sent and summed in bfloat16 or wider, within the bound.
No kernel may reach another device: no remote copies, remote signals or barrier semaphores. Data moves between devices by JAX's collectives and lax.ppermute only.
A program may use at most 64 MiB of HBM per device.

v0:
```python
import jax
import jax.numpy as jnp
from jax import lax
from jax.sharding import PartitionSpec as P

HEADS = 16
CONTRASTS = 4


def split_exact(value, upward):
    high = value.astype(jnp.bfloat16)
    rest = value - high.astype(jnp.float32)
    if upward:
        rest = rest + jnp.abs(rest) * 2.0 ** (-8)
    low = rest.astype(jnp.bfloat16)
    return (high, low)


def joined_rows(tokens, patch_of_row, contrast_gain, cycle_size, my_index):
    tok_rows, model_width = tokens.shape
    per_peer = tok_rows // cycle_size
    patches_dev = tok_rows // CONTRASTS
    all_ids = lax.all_gather(patch_of_row, "blk", tiled=True)
    received = lax.all_to_all(
        tokens.reshape(per_peer, cycle_size, model_width),
        "blk",
        split_axis=1,
        concat_axis=1,
        tiled=True,
    )
    received_ids = jnp.transpose(
        lax.dynamic_index_in_dim(
            all_ids.reshape(cycle_size, per_peer, cycle_size), my_index, axis=2, keepdims=False
        )
    )
    source_dev = lax.broadcasted_iota(jnp.int32, (per_peer, cycle_size), 1)
    row_step = lax.broadcasted_iota(jnp.int32, (per_peer, cycle_size), 0)
    slot_index = source_dev * tok_rows + my_index + cycle_size * row_step
    contrast_id = slot_index // (patches_dev * cycle_size)
    target_row = (contrast_id * patches_dev + received_ids - my_index * patches_dev).reshape(
        tok_rows
    )
    inverse = (
        jnp.zeros((tok_rows,), jnp.int32).at[target_row].set(jnp.arange(tok_rows, dtype=jnp.int32))
    )
    arranged = received.reshape(tok_rows, model_width)[inverse].reshape(
        CONTRASTS, patches_dev, model_width
    )
    return jnp.sum(
        arranged.astype(jnp.float32) * contrast_gain.astype(jnp.float32)[:, None, :], axis=0
    )


def local(tokens, patch_of_row, latents, contrast_gain, norm_gain, w_query, w_key, w_value, w_out):
    cycle_size = lax.axis_size("blk")
    my_index = lax.axis_index("blk")
    model_width = tokens.shape[1]
    head_count = HEADS
    head_width = model_width // head_count
    lat_rows = latents.shape[0]
    queries = (
        jnp.dot(latents, w_query, preferred_element_type=jnp.float32) * head_width ** (-0.5)
    ).astype(jnp.bfloat16)
    all_queries = lax.all_gather(queries, "blk", tiled=True)
    all_lat = all_queries.shape[0]
    joined = joined_rows(tokens, patch_of_row, contrast_gain, cycle_size, my_index)
    patches_dev = joined.shape[0]
    inverse_rms = lax.rsqrt(jnp.mean(joined * joined, axis=-1, keepdims=True) + 1e-05)
    normed = (joined * inverse_rms * norm_gain.astype(jnp.float32)).astype(jnp.bfloat16)
    key_rows = jnp.dot(normed, w_key, preferred_element_type=jnp.float32).astype(jnp.bfloat16)
    value_rows = jnp.dot(normed, w_value, preferred_element_type=jnp.float32).astype(jnp.bfloat16)
    key_heads = key_rows.reshape(patches_dev, head_count, head_width)
    value_heads = value_rows.reshape(patches_dev, head_count, head_width)
    query_heads = all_queries.reshape(all_lat, head_count, head_width)
    scores = jnp.einsum("lhd,khd->lhk", query_heads, key_heads, preferred_element_type=jnp.float32)
    maxima = jnp.max(scores, axis=-1)
    max_high, max_low = split_exact(maxima, True)
    shift = max_high.astype(jnp.float32) + max_low.astype(jnp.float32)
    weights = jnp.exp(scores - shift[..., None])
    totals = jnp.sum(weights, axis=-1)
    tot_high, tot_low = split_exact(totals, False)
    summed = jnp.einsum(
        "lhk,khd->lhd",
        weights.astype(jnp.bfloat16),
        value_heads,
        preferred_element_type=jnp.float32,
    )
    stats = jnp.stack([max_high, max_low, tot_high, tot_low], axis=-1).reshape(
        cycle_size, lat_rows, head_count * 4
    )
    payload = jnp.concatenate(
        [summed.astype(jnp.bfloat16).reshape(cycle_size, lat_rows, model_width), stats], axis=-1
    )
    gathered = lax.all_to_all(payload, "blk", split_axis=0, concat_axis=0, tiled=True)
    part_sums = (
        gathered[:, :, :model_width]
        .astype(jnp.float32)
        .reshape(cycle_size, lat_rows, head_count, head_width)
    )
    part_stats = (
        gathered[:, :, model_width:]
        .astype(jnp.float32)
        .reshape(cycle_size, lat_rows, head_count, 4)
    )
    part_max = part_stats[..., 0] + part_stats[..., 1]
    part_tot = part_stats[..., 2] + part_stats[..., 3]
    top = jnp.max(part_max, axis=0)
    factor = jnp.exp(part_max - top[None])
    total = jnp.sum(part_tot * factor, axis=0)
    accum = jnp.sum(part_sums * factor[..., None], axis=0)
    attended = (accum / total[..., None]).reshape(lat_rows, model_width).astype(jnp.bfloat16)
    mixed = latents.astype(jnp.float32) + jnp.dot(
        attended, w_out, preferred_element_type=jnp.float32
    )
    return mixed.astype(jnp.bfloat16)


def solution(mesh):
    in_specs = (
        P(("grp", "blk"), None),
        P(("grp", "blk")),
        P("blk", None),
        P(),
        P(),
        P(),
        P(),
        P(),
        P(),
    )
    out_specs = P(("grp", "blk"), None)
    return jax.shard_map(local, mesh=mesh, in_specs=in_specs, out_specs=out_specs, check_vma=False)
```

profile of v0, /device:TPU:0, one launch (start us, length us, event | category | flops | bytes accessed | tf_op | source)
XLA Modules:
  0.0 122.3 jit_solution(12066292924014967609)
XLA Ops:
  0.0 0.0 copy-start
  0.0 0.0 copy-start.7
  0.0 0.0 copy-start.6
  0.0 0.0 copy-start.8
  0.0 0.0 copy-start.5
  0.0 3.0 %copy.62 = bf16[32,16,1024]{2,0,1:T(8,128)(2,1)} copy(bf16[32,16,1024]{2,1,0:T(8,128)(2,1)} %bitcast.59) | data formatting | bytes 2097152 | tf_op jit(solution)/shard_map/reshape | solution.py:25
  3.0 7.4 %all-to-all-start = ((bf16[32,16,1024]{2,0,1:T(8,128)(2,1)}), bf16[32,16,1024]{2,0,1:T(8,128)(2,1)}, u32[]{:S(2)}, u32[]{:S(2)}) async-start(bf16[32,16,1024]{2,0,1:T(8,128)(2,1)} %copy.62), calls=%async_computation | async-start | bytes 2097152 | tf_op jit(solution)/shard_map/all_to_all | solution.py:24
  10.5 0.0 copy-done.7
  10.5 0.0 copy-done.6
  10.5 0.0 copy-done.8
  10.5 33.5 %all-gather = s32[16,1,512]{2,1,0:T(1,128)S(1)} all-gather(s32[1,1,512]{2,1,0:T(1,128)S(1)} %bitcast.62), channel_id=1, replica_groups=mesh['grp'=2,'blk'=16] {'blk'}, dimensions={0}, use_global_device_ids=true | all-gather | bytes 34816 | tf_op jit(solution)/shard_map/all_gather | solution.py:23
  44.1 0.1 reduce.2
  44.1 0.1 reshape.140
  44.3 0.5 dynamic-slice_reduce_fusion
  44.8 0.1 fusion.16
  44.8 0.1 copy.64
  44.9 0.1 reshape.141
  45.0 0.0 copy-done.5
  45.0 2.0 %fusion.5 = bf16[16,1024]{1,0:T(8,128)(2,1)S(1)} fusion(bf16[16,1024]{1,0:T(8,128)(2,1)S(1)} %copy-done.5, bf16[1024,1024]{1,0:T(8,128)(2,1)} %param.14), kind=kOutput, calls=%fused_computation.15 | convolution fusion | flops 33587200 | bytes 2162688 | tf_op jit(solution)/shard_map/dot_general | solution.py:62
  47.0 22.9 %all_gather.7 = bf16[256,1024]{1,0:T(8,128)(2,1)S(1)} all-gather(bf16[16,1024]{1,0:T(8,128)(2,1)S(1)} %fusion.5), channel_id=1, replica_groups=mesh['grp'=2,'blk'=16] {'blk'}, dimensions={0}, use_global_device_ids=true | all-gather | bytes 557056 | tf_op jit(solution)/shard_map/all_gather | solution.py:64
  69.9 1.0 copy.67
  70.9 2.4 %scatter_custom_fusion = s32[512]{0:T(512)S(1)} fusion(s32[512]{0:T(512)S(1)} %bitcast.63, s32[512]{0:T(512)S(1)} %iota.19, s32[]{:T(128)} %constant.15.clone.1), kind=kCustom, calls=%fused_computation.59 | custom fusion | bytes 2052 | tf_op jit(solution)/shard_map/scatter | solution.py:44
  73.4 0.0 all-to-all-done
  73.4 1.8 %copy.63 = bf16[32,16,1024]{2,1,0:T(8,128)(2,1)S(1)} copy(bf16[32,16,1024]{2,0,1:T(8,128)(2,1)} %all-to-all-done) | data formatting | bytes 2097152 | tf_op jit(solution)/shard_map/all_to_all | solution.py:24
  75.2 2.8 %gather_fusion = bf16[512,1024]{1,0:T(8,128)(2,1)} fusion(bf16[512,1024]{1,0:T(8,128)(2,1)S(1)} %bitcast.53, s32[1024]{0:T(1024)S(1)} %pad_clamp_fusion), kind=kCustom, calls=%fused_computation | custom fusion | bytes 2099200 | tf_op jit(solution)/shard_map/gather | solution.py:46
  78.0 1.5 %fusion = f32[128,1024]{1,0:T(8,128)S(1)} fusion(bf16[4,128,1024]{2,1,0:T(8,128)(2,1)} %bitcast.57, f32[4,1024]{1,0:T(4,128)S(1)} %convert_element_type.140), kind=kLoop, calls=%fused_computation.3 | loop fusion | flops 1441792 | bytes 1589248 | tf_op jit(solution)/shard_map/reduce_sum | solution.py:49
  79.5 0.0 copy-start.4
  79.5 0.1 multiply_reduce_fusion.1
  79.6 0.0 copy-done
  79.6 0.5 convolution_convert_fusion.1
  80.1 0.8 copy.66
  81.0 0.0 copy-done.4
  81.0 0.0 copy-start.3
  81.0 1.6 %bitcast_reduce_fusion = (f32[256,16]{0,1:T(8,128)S(1)}, f32[16,128,256]{2,1,0:T(8,128)S(1)}) fusion(bf16[128,16,64]{0,2,1:T(8,128)(2,1)} %bitcast.60, bf16[256,16,64]{0,2,1:T(8,128)(2,1)S(1)} %bitcast.58), kind=kOutput, calls=%fused_computation.5 | convolution fusion | flops 67629056 | bytes 2899968 | tf_op jit(solution)/shard_map/lhd,khd->lhk/dot_general | solution.py:75
  82.6 0.0 copy-start.1
  82.6 1.3 %copy-done.1 = f32[16,128,256]{2,1,0:T(8,128)} copy-done((f32[16,128,256]{2,1,0:T(8,128)}, f32[16,128,256]{2,1,0:T(8,128)S(1)}, u32[]{:S(2)}) %copy-start.1) | copy-done | bytes 2097176
  83.9 0.3 fusion.2
  84.3 0.0 copy-done.3
  84.3 0.5 convolution_convert_fusion.2
  84.8 0.2 copy.65
  85.0 2.9 %fusion.4 = bf16[256,16,64]{0,2,1:T(8,128)(2,1)} fusion(bf16[128,16,64]{0,2,1:T(8,128)(2,1)S(1)} %bitcast.61, f32[16,128,256]{2,1,0:T(8,128)} %copy-done.1, f32[256,16]{0,1:T(8,128)S(1)} %convert_add_fusion), kind=kOutput, calls=%fused_computation.10 | convolution fusion | flops 68419584 | bytes 2899968 | tf_op jit(solution)/shard_map/lhk,khd->lhd/dot_general | solution.py:82
  87.9 0.1 pad_maximum_fusion.1
  88.0 0.2 reshape.146
  88.2 0.3 copy.70
  88.5 2.0 %copy.69 = bf16[256,16,64]{2,1,0:T(8,128)(2,1)S(1)} copy(bf16[256,16,64]{0,2,1:T(8,128)(2,1)} %fusion.4) | data formatting | bytes 1048576 | tf_op jit(solution)/shard_map/convert_element_type | solution.py:92
  90.5 1.5 %reshape.145 = bf16[16,16,1024]{2,1,0:T(8,128)(2,1)} reshape(bf16[256,16,64]{2,1,0:T(8,128)(2,1)S(1)} %copy.69) | data formatting | bytes 1048576 | tf_op jit(solution)/shard_map/reshape | solution.py:92
  92.0 1.1 pad_maximum_fusion
  93.1 19.8 %all_to_all.10 = bf16[16,16,1088]{2,1,0:T(8,128)(2,1)S(1)} all-to-all(bf16[16,16,1088]{2,1,0:T(8,128)(2,1)S(1)} %pad_maximum_fusion), channel_id=1, replica_groups=mesh['grp'=2,'blk'=16] {'blk'}, dimensions={0} | all-to-all | bytes 1114112 | tf_op jit(solution)/shard_map/all_to_all | solution.py:94
  112.9 0.0 copy-start.2
  112.9 0.8 copy-done.2
  113.7 0.3 copy.71
  114.1 0.1 fusion.11
  114.2 0.1 copy.72
  114.3 0.1 copy.75
  114.4 0.1 div.35
  114.5 0.1 div.36
  114.6 2.0 %mul.113 = f32[16,16,16,64]{3,2,1,0:T(8,128)} broadcast(f32[16,16,16]{2,1,0:T(8,128)S(1)} %copy.72), dimensions={0,1,2} | broadcast | bytes 1064960 | tf_op jit(solution)/shard_map/mul | solution.py:110
  116.5 2.0 %mul.114 = f32[16,16,1024]{2,1,0:T(8,128)S(1)} reshape(f32[16,16,16,64]{3,2,1,0:T(8,128)} %mul.113) | data formatting | bytes 2097152 | tf_op jit(solution)/shard_map/mul | solution.py:110
  118.5 1.2 multiply_reduce_fusion
  119.7 2.6 %fusion.6 = bf16[16,1024]{1,0:T(8,128)(2,1)} fusion(bf16[1024,1024]{1,0:T(8,128)(2,1)} %param.17, bf16[16,1024]{1,0:T(8,128)(2,1)S(1)} %copy-done.5, f32[16,1024]{1,0:T(8,128)S(1)} %multiply_reduce_fusion, f32[16,1024]{1,0:T(8,128)S(1)} %div.36), kind=kOutput, calls=%fused_computation.16 | convolution fusion | flops 33636352 | bytes 2293760 | tf_op jit(solution)/shard_map/dot_general | solution.py:112
  (16 shorter events, 0.2 us)
Async XLA Ops:
  0.0 79.6 %copy-start = (bf16[1024,1024]{1,0:T(8,128)(2,1)S(1)}, bf16[1024,1024]{1,0:T(8,128)(2,1)}, u32[]{:S(2)}) copy-start(bf16[1024,1024]{1,0:T(8,128)(2,1)} %param.15) | copy-start | bytes 6291460
  0.0 10.5 %copy-start.7 = (bf16[1024]{0:T(1024)(128)(2,1)S(1)}, bf16[1024]{0:T(1024)(128)(2,1)}, u32[]{:S(2)}) copy-start(bf16[1024]{0:T(1024)(128)(2,1)} %param.13) | copy-start | bytes 6148
  0.0 10.5 %copy-start.6 = (bf16[4,1024]{1,0:T(4,128)(2,1)S(1)}, bf16[4,1024]{1,0:T(4,128)(2,1)}, u32[]{:S(2)}) copy-start(bf16[4,1024]{1,0:T(4,128)(2,1)} %param.12) | copy-start | bytes 24580
  0.0 10.5 %copy-start.8 = (s32[512]{0:T(512)S(1)}, s32[512]{0:T(512)}, u32[]{:S(2)}) copy-start(s32[512]{0:T(512)} %param.10) | copy-start | bytes 6148
  0.0 45.0 %copy-start.5 = (bf16[16,1024]{1,0:T(8,128)(2,1)S(1)}, bf16[16,1024]{1,0:T(8,128)(2,1)}, u32[]{:S(2)}) copy-start(bf16[16,1024]{1,0:T(8,128)(2,1)} %param.11) | copy-start | bytes 98308
  3.0 70.4 %all-to-all-start = ((bf16[32,16,1024]{2,0,1:T(8,128)(2,1)}), bf16[32,16,1024]{2,0,1:T(8,128)(2,1)}, u32[]{:S(2)}, u32[]{:S(2)}) async-start(bf16[32,16,1024]{2,0,1:T(8,128)(2,1)} %copy.62), calls=%async_computation | async-start | bytes 2097152 | tf_op jit(solution)/shard_map/all_to_all | solution.py:24
  79.5 1.5 %copy-start.4 = (bf16[256,1024]{0,1:T(8,128)(2,1)S(1)}, bf16[256,1024]{0,1:T(8,128)(2,1)}, u32[]{:S(2)}) copy-start(bf16[256,1024]{0,1:T(8,128)(2,1)} %copy.67) | copy-start | bytes 1572868
  81.0 3.3 %copy-start.3 = (bf16[1024,1024]{1,0:T(8,128)(2,1)S(1)}, bf16[1024,1024]{1,0:T(8,128)(2,1)}, u32[]{:S(2)}) copy-start(bf16[1024,1024]{1,0:T(8,128)(2,1)} %param.16) | copy-start | bytes 6291460
  82.6 1.4 %copy-start.1 = (f32[16,128,256]{2,1,0:T(8,128)}, f32[16,128,256]{2,1,0:T(8,128)S(1)}, u32[]{:S(2)}) copy-start(f32[16,128,256]{2,1,0:T(8,128)S(1)} %get-tuple-element.6) | copy-start | bytes 6291460
  112.9 0.8 copy-start.2
where the time goes:
time: 123 us; the launch traced here: 122 us
  blocking collectives  76.3 us (62%)
  local copies, waits for them, and re-layouts  23.5 us (19%)
  matrix products  10.1 us (8%)
  starting transfers between devices  7.44 us (6%)
  other arithmetic  4.65 us (4%)
    all_gather x1, blocking collectives, joined_rows(): all_ids = lax.all_gather(patch_of_row, 'blk', tiled=True)  33.5 us
    all_gather x1, blocking collectives, local(): all_queries = lax.all_gather(queries, 'blk', tiled=True)  22.9 us
    all_to_all x1, blocking collectives, local(): lax.all_to_all(payload, 'blk', split_axis=0, concat_axis=0, tiled=True)  19.8 us
    all_to_all x1, starting transfers between devices, joined_rows(): lax.all_to_all(tokens.reshape(per_peer, cycle_size, model_width), 'blk',...  7.44 us
    mul x3, local copies, waits for them, and re-layouts, local(): accum = jnp.sum(part_sums * factor[..., None], axis=0)  4.08 us
    reshape x1, local copies, waits for them, and re-layouts, joined_rows(): tokens.reshape(per_peer, cycle_size, model_width)  2.98 us
    dot_general x1, matrix products, local(): jnp.einsum('lhk,khd->lhd', weights.astype(jnp.bfloat16), value_heads, pre...  2.89 us
    gather x1, local copies, waits for them, and re-layouts, joined_rows(): received.reshape(tok_rows, model_width)[inverse]  2.79 us
  transfers between devices with their start and end apart: 1, of which 0 were waited for; matrix products, arithmetic and copies ran while one was open for 5% of the time, Pallas kernels for 0%

commit v1 on v0

--- a/solution.py
+++ b/solution.py
@@ -17,10 +17,29 @@
 
 
 def joined_rows(tokens, patch_of_row, contrast_gain, cycle_size, my_index):
+
+    def plan_rails_up(a0):
+        across = "blk"
+        dev_count = lax.axis_size(across)
+        shelf = [(it, (it + 1) % dev_count) for it in range(dev_count)]
+
+        def floor_choose(all_rows):
+            if len(all_rows) == dev_count:
+                return all_rows
+            side_arr = lax.ppermute(all_rows[0], across, shelf)
+            vec_out = floor_choose([side_arr, *all_rows])
+            return vec_out
+
+        m_next = floor_choose([a0])
+        f_now = jnp.concatenate(m_next, axis=0)
+        long_array = lax.axis_index(across)
+        u_next = jnp.roll(f_now, (long_array + 1) * a0.shape[0], axis=0)
+        return u_next
+
     tok_rows, model_width = tokens.shape
     per_peer = tok_rows // cycle_size
     patches_dev = tok_rows // CONTRASTS
-    all_ids = lax.all_gather(patch_of_row, "blk", tiled=True)
+    all_ids = plan_rails_up(patch_of_row)
     received = lax.all_to_all(
         tokens.reshape(per_peer, cycle_size, model_width),
         "blk",

time: 123 us -> 174 us (1.41)
  waiting for transfers between devices: 0.01 us -> 88 us
  blocking collectives: 76.3 us -> 39.3 us
    ppermute x0 -> x15, waiting for transfers between devices: none -> 88 us  [floor_choose(): side_arr = lax.ppermute(all_rows[0], across, shelf)]
    all_gather x1 -> x0, blocking collectives: 33.5 us -> none  [joined_rows(): all_ids = lax.all_gather(patch_of_row, 'blk', tiled=True)]
    all_gather x1, blocking collectives: 22.9 us -> 19.4 us  [local(): all_queries = lax.all_gather(queries, 'blk', tiled=True)]
  transfers between devices with their start and end apart: 1 -> 16, of which waited for: 0 -> 13; matrix products, arithmetic and copies ran while one was open for 5% -> 5% of each run, Pallas kernels for 0% -> 0%
where the time goes in v1:
time: 174 us; the launch traced here: 173 us
  waiting for transfers between devices  88 us (51%)
  blocking collectives  39.3 us (23%)
  local copies, waits for them, and re-layouts  23.6 us (14%)
  matrix products  10 us (6%)
  starting transfers between devices  7.06 us (4%)
  other arithmetic  4.58 us (3%)
    ppermute x15, waiting for transfers between devices, floor_choose(): side_arr = lax.ppermute(all_rows[0], across, shelf)  88 us
    all_to_all x1, blocking collectives, local(): lax.all_to_all(payload, 'blk', split_axis=0, concat_axis=0, tiled=True)  19.8 us
    all_gather x1, blocking collectives, local(): all_queries = lax.all_gather(queries, 'blk', tiled=True)  19.4 us
    all_to_all x1, starting transfers between devices, joined_rows(): lax.all_to_all(tokens.reshape(per_peer, cycle_size, model_width), 'blk',...  6 us
    mul x3, local copies, waits for them, and re-layouts, local(): accum = jnp.sum(part_sums * factor[..., None], axis=0)  4.07 us
  transfers between devices with their start and end apart: 16, of which 13 were waited for; matrix products, arithmetic and copies ran while one was open for 5% of the time, Pallas kernels for 0%

profile of v1, /device:TPU:0, one launch (start us, length us, event | category | flops | bytes accessed | tf_op | source)
XLA Modules:
  0.0 173.2 jit_solution(5614786078349021345)
XLA Ops:
  0.0 0.5 collective-permute-start
  0.5 6.5 %collective-permute-done = s32[512]{0:T(512)S(1)} collective-permute-done((s32[512]{0:T(512)}, s32[512]{0:T(512)S(1)}, u32[]{:S(2)}, u32[]{:S(2)}) %collective-permute-start) | collective-permute-done | bytes 2080 | tf_op jit(solution)/shard_map/ppermute | solution.py:29
  6.9 5.7 %collective-permute-done.1 = s32[512]{0:T(512)S(1)} collective-permute-done((s32[512]{0:T(512)S(1)}, s32[512]{0:T(512)S(1)}, u32[]{:S(2)}, u32[]{:S(2)}) %collective-permute-start.1) | collective-permute-done | bytes 2080 | tf_op jit(solution)/shard_map/ppermute | solution.py:29
  12.6 0.0 collective-permute-start.2
  12.6 5.7 %collective-permute-done.2 = s32[512]{0:T(512)S(1)} collective-permute-done((s32[512]{0:T(512)S(1)}, s32[512]{0:T(512)S(1)}, u32[]{:S(2)}, u32[]{:S(2)}) %collective-permute-start.2) | collective-permute-done | bytes 2080 | tf_op jit(solution)/shard_map/ppermute | solution.py:29
  18.3 0.0 collective-permute-start.3
  18.3 5.7 %collective-permute-done.3 = s32[512]{0:T(512)S(1)} collective-permute-done((s32[512]{0:T(512)S(1)}, s32[512]{0:T(512)S(1)}, u32[]{:S(2)}, u32[]{:S(2)}) %collective-permute-start.3) | collective-permute-done | bytes 2080 | tf_op jit(solution)/shard_map/ppermute | solution.py:29
  24.1 5.7 %collective-permute-done.4 = s32[512]{0:T(512)S(1)} collective-permute-done((s32[512]{0:T(512)S(1)}, s32[512]{0:T(512)S(1)}, u32[]{:S(2)}, u32[]{:S(2)}) %collective-permute-start.4) | collective-permute-done | bytes 2080 | tf_op jit(solution)/shard_map/ppermute | solution.py:29
  29.8 5.7 %collective-permute-done.5 = s32[512]{0:T(512)S(1)} collective-permute-done((s32[512]{0:T(512)S(1)}, s32[512]{0:T(512)S(1)}, u32[]{:S(2)}, u32[]{:S(2)}) %collective-permute-start.5) | collective-permute-done | bytes 2080 | tf_op jit(solution)/shard_map/ppermute | solution.py:29
  35.5 0.0 collective-permute-start.6
  35.5 5.7 %collective-permute-done.6 = s32[512]{0:T(512)S(1)} collective-permute-done((s32[512]{0:T(512)S(1)}, s32[512]{0:T(512)S(1)}, u32[]{:S(2)}, u32[]{:S(2)}) %collective-permute-start.6) | collective-permute-done | bytes 2080 | tf_op jit(solution)/shard_map/ppermute | solution.py:29
  41.2 0.0 collective-permute-start.7
  41.2 5.7 %collective-permute-done.7 = s32[512]{0:T(512)S(1)} collective-permute-done((s32[512]{0:T(512)S(1)}, s32[512]{0:T(512)S(1)}, u32[]{:S(2)}, u32[]{:S(2)}) %collective-permute-start.7) | collective-permute-done | bytes 2080 | tf_op jit(solution)/shard_map/ppermute | solution.py:29
  46.9 5.7 %collective-permute-done.8 = s32[512]{0:T(512)S(1)} collective-permute-done((s32[512]{0:T(512)S(1)}, s32[512]{0:T(512)S(1)}, u32[]{:S(2)}, u32[]{:S(2)}) %collective-permute-start.8) | collective-permute-done | bytes 2080 | tf_op jit(solution)/shard_map/ppermute | solution.py:29
  52.6 0.0 collective-permute-start.9
  52.6 5.7 %collective-permute-done.9 = s32[512]{0:T(512)S(1)} collective-permute-done((s32[512]{0:T(512)S(1)}, s32[512]{0:T(512)S(1)}, u32[]{:S(2)}, u32[]{:S(2)}) %collective-permute-start.9) | collective-permute-done | bytes 2080 | tf_op jit(solution)/shard_map/ppermute | solution.py:29
  58.3 2.8 %copy.62 = bf16[32,16,1024]{2,0,1:T(8,128)(2,1)} copy(bf16[32,16,1024]{2,1,0:T(8,128)(2,1)} %bitcast.58) | data formatting | bytes 2097152 | tf_op jit(solution)/shard_map/reshape | solution.py:44
  61.1 6.0 %all-to-all-start = ((bf16[32,16,1024]{2,0,1:T(8,128)(2,1)}), bf16[32,16,1024]{2,0,1:T(8,128)(2,1)}, u32[]{:S(2)}, u32[]{:S(2)}) async-start(bf16[32,16,1024]{2,0,1:T(8,128)(2,1)} %copy.62), calls=%async_computation | async-start | bytes 2097152 | tf_op jit(solution)/shard_map/all_to_all | solution.py:43
  67.1 0.0 copy-start.7
  67.2 0.4 collective-permute-start.11
  67.6 2.0 %fusion.5 = bf16[16,1024]{1,0:T(8,128)(2,1)S(1)} fusion(bf16[16,1024]{1,0:T(8,128)(2,1)S(1)} %copy-done.5, bf16[1024,1024]{1,0:T(8,128)(2,1)} %param.14), kind=kOutput, calls=%fused_computation.15 | convolution fusion | flops 33587200 | bytes 2162688 | tf_op jit(solution)/shard_map/dot_general | solution.py:81
  69.6 20.0 %collective-permute-done.11 = s32[512]{0:T(512)S(1)} collective-permute-done((s32[512]{0:T(512)S(1)}, s32[512]{0:T(512)S(1)}, u32[]{:S(2)}, u32[]{:S(2)}) %collective-permute-start.11) | collective-permute-done | bytes 2080 | tf_op jit(solution)/shard_map/ppermute | solution.py:29
  89.6 19.4 %all_gather.3 = bf16[256,1024]{1,0:T(8,128)(2,1)S(1)} all-gather(bf16[16,1024]{1,0:T(8,128)(2,1)S(1)} %fusion.5), channel_id=1, replica_groups=mesh['grp'=2,'blk'=16] {'blk'}, dimensions={0}, use_global_device_ids=true | all-gather | bytes 557056 | tf_op jit(solution)/shard_map/all_gather | solution.py:83
  109.0 0.2 collective-permute-start.13
  109.2 5.5 %collective-permute-done.13 = s32[512]{0:T(512)S(1)} collective-permute-done((s32[512]{0:T(512)S(1)}, s32[512]{0:T(512)S(1)}, u32[]{:S(2)}, u32[]{:S(2)}) %collective-permute-start.13) | collective-permute-done | bytes 2080 | tf_op jit(solution)/shard_map/ppermute | solution.py:29
  114.8 1.0 copy.67
  115.8 4.6 %collective-permute-done.14 = s32[512]{0:T(512)S(1)} collective-permute-done((s32[512]{0:T(512)S(1)}, s32[512]{0:T(512)S(1)}, u32[]{:S(2)}, u32[]{:S(2)}) %collective-permute-start.14) | collective-permute-done | bytes 2080 | tf_op jit(solution)/shard_map/ppermute | solution.py:29
  120.9 0.1 dynamic_slice.8
  120.9 0.1 reshape.140
  121.1 0.5 dynamic-slice_reduce_fusion
  121.5 0.1 fusion.16
  121.6 0.1 copy.64
  121.7 0.1 reshape.141
  121.8 2.4 %scatter_custom_fusion = s32[512]{0:T(512)S(1)} fusion(s32[512]{0:T(512)S(1)} %bitcast.61, s32[512]{0:T(512)S(1)} %iota.19, s32[]{:T(128)} %constant.32.clone.1), kind=kCustom, calls=%fused_computation.91 | custom fusion | bytes 2052 | tf_op jit(solution)/shard_map/scatter | solution.py:63
  124.3 1.8 %copy.63 = bf16[32,16,1024]{2,1,0:T(8,128)(2,1)S(1)} copy(bf16[32,16,1024]{2,0,1:T(8,128)(2,1)} %all-to-all-done) | data formatting | bytes 2097152 | tf_op jit(solution)/shard_map/all_to_all | solution.py:43
  126.1 2.8 %gather_fusion = bf16[512,1024]{1,0:T(8,128)(2,1)} fusion(bf16[512,1024]{1,0:T(8,128)(2,1)S(1)} %bitcast.52, s32[1024]{0:T(1024)S(1)} %pad_clamp_fusion), kind=kCustom, calls=%fused_computation | custom fusion | bytes 2099200 | tf_op jit(solution)/shard_map/gather | solution.py:65
  128.9 1.5 fusion
  130.4 0.1 multiply_reduce_fusion.1
  130.5 0.5 convolution_convert_fusion.1
  131.0 0.8 copy.66
  131.9 1.6 bitcast_reduce_fusion
  133.5 1.3 copy-done.1
  134.8 0.3 fusion.2
  135.2 0.5 convolution_convert_fusion.2
  135.7 0.2 copy.65
  135.9 2.9 %fusion.4 = bf16[256,16,64]{0,2,1:T(8,128)(2,1)} fusion(bf16[128,16,64]{0,2,1:T(8,128)(2,1)S(1)} %bitcast.60, f32[16,128,256]{2,1,0:T(8,128)} %copy-done.1, f32[256,16]{0,1:T(8,128)S(1)} %convert_add_fusion), kind=kOutput, calls=%fused_computation.10 | convolution fusion | flops 68419584 | bytes 2899968 | tf_op jit(solution)/shard_map/lhk,khd->lhd/dot_general | solution.py:101
  138.7 0.1 pad_maximum_fusion.1
  138.8 0.2 reshape.146
  139.1 0.3 copy.70
  139.3 2.0 %copy.69 = bf16[256,16,64]{2,1,0:T(8,128)(2,1)S(1)} copy(bf16[256,16,64]{0,2,1:T(8,128)(2,1)} %fusion.4) | data formatting | bytes 1048576 | tf_op jit(solution)/shard_map/convert_element_type | solution.py:111
  141.3 1.5 reshape.145
  142.8 1.1 pad_maximum_fusion
  143.9 19.8 %all_to_all.10 = bf16[16,16,1088]{2,1,0:T(8,128)(2,1)S(1)} all-to-all(bf16[16,16,1088]{2,1,0:T(8,128)(2,1)S(1)} %pad_maximum_fusion), channel_id=1, replica_groups=mesh['grp'=2,'blk'=16] {'blk'}, dimensions={0} | all-to-all | bytes 1114112 | tf_op jit(solution)/shard_map/all_to_all | solution.py:113
  163.8 0.8 copy-done.2
  164.6 0.3 copy.71
  164.9 0.1 fusion.11
  165.0 0.1 copy.72
  165.2 0.1 copy.75
  165.2 0.1 div.35
  165.3 0.1 div.36
  165.4 1.9 %mul.117 = f32[16,16,16,64]{3,2,1,0:T(8,128)} broadcast(f32[16,16,16]{2,1,0:T(8,128)S(1)} %copy.72), dimensions={0,1,2} | broadcast | bytes 1064960 | tf_op jit(solution)/shard_map/mul | solution.py:129
  167.4 2.0 %mul.118 = f32[16,16,1024]{2,1,0:T(8,128)S(1)} reshape(f32[16,16,16,64]{3,2,1,0:T(8,128)} %mul.117) | data formatting | bytes 2097152 | tf_op jit(solution)/shard_map/mul | solution.py:129
  169.4 1.2 multiply_reduce_fusion
  170.6 2.6 %fusion.6 = bf16[16,1024]{1,0:T(8,128)(2,1)} fusion(bf16[1024,1024]{1,0:T(8,128)(2,1)} %param.17, bf16[16,1024]{1,0:T(8,128)(2,1)S(1)} %copy-done.5, f32[16,1024]{1,0:T(8,128)S(1)} %multiply_reduce_fusion, f32[16,1024]{1,0:T(8,128)S(1)} %div.36), kind=kOutput, calls=%fused_computation.16 | convolution fusion | flops 33636352 | bytes 2293760 | tf_op jit(solution)/shard_map/dot_general | solution.py:131
  (74 shorter events, 0.4 us)
Async XLA Ops:
  0.0 130.5 %copy-start = (bf16[1024,1024]{1,0:T(8,128)(2,1)S(1)}, bf16[1024,1024]{1,0:T(8,128)(2,1)}, u32[]{:S(2)}) copy-start(bf16[1024,1024]{1,0:T(8,128)(2,1)} %param.15) | copy-start | bytes 6291460
  0.0 6.9 %collective-permute-start = (s32[512]{0:T(512)}, s32[512]{0:T(512)S(1)}, u32[]{:S(2)}, u32[]{:S(2)}) collective-permute-start(s32[512]{0:T(512)} %param.10), channel_id=1, source_target_pairs={{0,1},{1,2},{2,3},{3,4},{4,5},{5,6},{6,7},{7,8},{8,9},{9,10},{10,1... | collective-permute-start | bytes 6152 | tf_op jit(solution)/shard_map/ppermute | solution.py:29
  6.9 5.7 %collective-permute-start.1 = (s32[512]{0:T(512)S(1)}, s32[512]{0:T(512)S(1)}, u32[]{:S(2)}, u32[]{:S(2)}) collective-permute-start(s32[512]{0:T(512)S(1)} %collective-permute-done), channel_id=1, source_target_pairs={{0,1},{1,2},{2,3},{3,4},{4,5},{5,6},{6,7},{7,8},{8,9},{9,10},{10,1... | collective-permute-start | bytes 6152 | tf_op jit(solution)/shard_map/ppermute | solution.py:29
  12.6 5.7 %collective-permute-start.2 = (s32[512]{0:T(512)S(1)}, s32[512]{0:T(512)S(1)}, u32[]{:S(2)}, u32[]{:S(2)}) collective-permute-start(s32[512]{0:T(512)S(1)} %collective-permute-done.1), channel_id=1, source_target_pairs={{0,1},{1,2},{2,3},{3,4},{4,5},{5,6},{6,7},{7,8},{8,9},{9,10},{10,1... | collective-permute-start | bytes 6152 | tf_op jit(solution)/shard_map/ppermute | solution.py:29
  18.3 5.7 %collective-permute-start.3 = (s32[512]{0:T(512)S(1)}, s32[512]{0:T(512)S(1)}, u32[]{:S(2)}, u32[]{:S(2)}) collective-permute-start(s32[512]{0:T(512)S(1)} %collective-permute-done.2), channel_id=1, source_target_pairs={{0,1},{1,2},{2,3},{3,4},{4,5},{5,6},{6,7},{7,8},{8,9},{9,10},{10,1... | collective-permute-start | bytes 6152 | tf_op jit(solution)/shard_map/ppermute | solution.py:29
  24.0 5.7 %collective-permute-start.4 = (s32[512]{0:T(512)S(1)}, s32[512]{0:T(512)S(1)}, u32[]{:S(2)}, u32[]{:S(2)}) collective-permute-start(s32[512]{0:T(512)S(1)} %collective-permute-done.3), channel_id=1, source_target_pairs={{0,1},{1,2},{2,3},{3,4},{4,5},{5,6},{6,7},{7,8},{8,9},{9,10},{10,1... | collective-permute-start | bytes 6152 | tf_op jit(solution)/shard_map/ppermute | solution.py:29
  29.8 5.7 %collective-permute-start.5 = (s32[512]{0:T(512)S(1)}, s32[512]{0:T(512)S(1)}, u32[]{:S(2)}, u32[]{:S(2)}) collective-permute-start(s32[512]{0:T(512)S(1)} %collective-permute-done.4), channel_id=1, source_target_pairs={{0,1},{1,2},{2,3},{3,4},{4,5},{5,6},{6,7},{7,8},{8,9},{9,10},{10,1... | collective-permute-start | bytes 6152 | tf_op jit(solution)/shard_map/ppermute | solution.py:29
  35.5 5.7 %collective-permute-start.6 = (s32[512]{0:T(512)S(1)}, s32[512]{0:T(512)S(1)}, u32[]{:S(2)}, u32[]{:S(2)}) collective-permute-start(s32[512]{0:T(512)S(1)} %collective-permute-done.5), channel_id=1, source_target_pairs={{0,1},{1,2},{2,3},{3,4},{4,5},{5,6},{6,7},{7,8},{8,9},{9,10},{10,1... | collective-permute-start | bytes 6152 | tf_op jit(solution)/shard_map/ppermute | solution.py:29
  41.2 5.7 %collective-permute-start.7 = (s32[512]{0:T(512)S(1)}, s32[512]{0:T(512)S(1)}, u32[]{:S(2)}, u32[]{:S(2)}) collective-permute-start(s32[512]{0:T(512)S(1)} %collective-permute-done.6), channel_id=1, source_target_pairs={{0,1},{1,2},{2,3},{3,4},{4,5},{5,6},{6,7},{7,8},{8,9},{9,10},{10,1... | collective-permute-start | bytes 6152 | tf_op jit(solution)/shard_map/ppermute | solution.py:29
  46.9 5.7 %collective-permute-start.8 = (s32[512]{0:T(512)S(1)}, s32[512]{0:T(512)S(1)}, u32[]{:S(2)}, u32[]{:S(2)}) collective-permute-start(s32[512]{0:T(512)S(1)} %collective-permute-done.7), channel_id=1, source_target_pairs={{0,1},{1,2},{2,3},{3,4},{4,5},{5,6},{6,7},{7,8},{8,9},{9,10},{10,1... | collective-permute-start | bytes 6152 | tf_op jit(solution)/shard_map/ppermute | solution.py:29
  52.6 5.7 %collective-permute-start.9 = (s32[512]{0:T(512)S(1)}, s32[512]{0:T(512)S(1)}, u32[]{:S(2)}, u32[]{:S(2)}) collective-permute-start(s32[512]{0:T(512)S(1)} %collective-permute-done.8), channel_id=1, source_target_pairs={{0,1},{1,2},{2,3},{3,4},{4,5},{5,6},{6,7},{7,8},{8,9},{9,10},{10,1... | collective-permute-start | bytes 6152 | tf_op jit(solution)/shard_map/ppermute | solution.py:29
  58.3 8.9 %collective-permute-start.10 = (s32[512]{0:T(512)S(1)}, s32[512]{0:T(512)S(1)}, u32[]{:S(2)}, u32[]{:S(2)}) collective-permute-start(s32[512]{0:T(512)S(1)} %collective-permute-done.9), channel_id=1, source_target_pairs={{0,1},{1,2},{2,3},{3,4},{4,5},{5,6},{6,7},{7,8},{8,9},{9,10},{10,1... | collective-permute-start | bytes 6152 | tf_op jit(solution)/shard_map/ppermute | solution.py:29
  58.3 9.3 %copy-start.5 = (bf16[16,1024]{1,0:T(8,128)(2,1)S(1)}, bf16[16,1024]{1,0:T(8,128)(2,1)}, u32[]{:S(2)}) copy-start(bf16[16,1024]{1,0:T(8,128)(2,1)} %param.11) | copy-start | bytes 98308
  61.1 53.6 %copy-start.8 = (bf16[1024]{0:T(1024)(128)(2,1)S(1)}, bf16[1024]{0:T(1024)(128)(2,1)}, u32[]{:S(2)}) copy-start(bf16[1024]{0:T(1024)(128)(2,1)} %param.13) | copy-start | bytes 6148
  61.1 53.7 %copy-start.6 = (bf16[4,1024]{1,0:T(4,128)(2,1)S(1)}, bf16[4,1024]{1,0:T(4,128)(2,1)}, u32[]{:S(2)}) copy-start(bf16[4,1024]{1,0:T(4,128)(2,1)} %param.12) | copy-start | bytes 24580
  61.1 63.1 %all-to-all-start = ((bf16[32,16,1024]{2,0,1:T(8,128)(2,1)}), bf16[32,16,1024]{2,0,1:T(8,128)(2,1)}, u32[]{:S(2)}, u32[]{:S(2)}) async-start(bf16[32,16,1024]{2,0,1:T(8,128)(2,1)} %copy.62), calls=%async_computation | async-start | bytes 2097152 | tf_op jit(solution)/shard_map/all_to_all | solution.py:43
  67.1 53.5 %copy-start.7 = (s32[512]{0:T(512)S(1)}, s32[512]{0:T(512)}, u32[]{:S(2)}) copy-start(s32[512]{0:T(512)} %param.10) | copy-start | bytes 6148
  67.2 22.4 %collective-permute-start.11 = (s32[512]{0:T(512)S(1)}, s32[512]{0:T(512)S(1)}, u32[]{:S(2)}, u32[]{:S(2)}) collective-permute-start(s32[512]{0:T(512)S(1)} %collective-permute-done.10), channel_id=1, source_target_pairs={{0,1},{1,2},{2,3},{3,4},{4,5},{5,6},{6,7},{7,8},{8,9},{9,10},{10,1... | collective-permute-start | bytes 6152 | tf_op jit(solution)/shard_map/ppermute | solution.py:29
  89.6 19.4 %collective-permute-start.12 = (s32[512]{0:T(512)S(1)}, s32[512]{0:T(512)S(1)}, u32[]{:S(2)}, u32[]{:S(2)}) collective-permute-start(s32[512]{0:T(512)S(1)} %collective-permute-done.11), channel_id=1, source_target_pairs={{0,1},{1,2},{2,3},{3,4},{4,5},{5,6},{6,7},{7,8},{8,9},{9,10},{10,1... | collective-permute-start | bytes 6152 | tf_op jit(solution)/shard_map/ppermute | solution.py:29
  109.0 5.7 %collective-permute-start.13 = (s32[512]{0:T(512)S(1)}, s32[512]{0:T(512)S(1)}, u32[]{:S(2)}, u32[]{:S(2)}) collective-permute-start(s32[512]{0:T(512)S(1)} %collective-permute-done.12), channel_id=1, source_target_pairs={{0,1},{1,2},{2,3},{3,4},{4,5},{5,6},{6,7},{7,8},{8,9},{9,10},{10,1... | collective-permute-start | bytes 6152 | tf_op jit(solution)/shard_map/ppermute | solution.py:29
  114.7 5.7 %collective-permute-start.14 = (s32[512]{0:T(512)S(1)}, s32[512]{0:T(512)S(1)}, u32[]{:S(2)}, u32[]{:S(2)}) collective-permute-start(s32[512]{0:T(512)S(1)} %collective-permute-done.13), channel_id=1, source_target_pairs={{0,1},{1,2},{2,3},{3,4},{4,5},{5,6},{6,7},{7,8},{8,9},{9,10},{10,1... | collective-permute-start | bytes 6152 | tf_op jit(solution)/shard_map/ppermute | solution.py:29
  130.4 1.5 copy-start.4
  131.9 3.3 %copy-start.3 = (bf16[1024,1024]{1,0:T(8,128)(2,1)S(1)}, bf16[1024,1024]{1,0:T(8,128)(2,1)}, u32[]{:S(2)}) copy-start(bf16[1024,1024]{1,0:T(8,128)(2,1)} %param.16) | copy-start | bytes 6291460
  133.5 1.3 copy-start.1
  163.8 0.8 copy-start.2
